TPU v7x, 256 devices: a whole 4x4x8 slice. The times are simulated.
256 devices in a mesh: tok: 16 (over z, core), tp: 16 (over x, y).
Axes of the slice: x: 4, y: 4, z: 8, core: 2. Of those that a mesh axis runs over, the one named last changes fastest.
Arguments:
- hidden_states: bfloat16 [32768, 1024], P(('tok', 'tp')), may hold values from -40 to 40
- first_gain: float32 [1024], replicated, may hold values from 0.1 to 1.9
- second_gain: float32 [1024], replicated, may hold values from 0.1 to 1.9
- w_query: bfloat16 [1024, 1024], P(None, 'tp'), may hold values from -1 to 1
- w_keyval: bfloat16 [1024, 1024], replicated, may hold values from -0.375 to 0.375
- w_out: bfloat16 [1024, 1024], P('tp'), may hold values from -0.75 to 0.75
- kv_cache: bfloat16 [384, 128, 1024], P('tok'), may hold values from -310 to 310
- page_table: int32 [32, 16], P('tok'), may hold values from 0 to 383, as said below
- cached_len: int32 [32], P('tok'), may hold values from 128 to 2048, as said below
- expert_ids: int32 [32768, 8], P(('tok', 'tp')), may hold values from 0 to 31, all different within a row; in each aligned block of 128 rows (0 to 127, 128 to 255, ...) at most 64 rows name the same one
- gate_weights: float32 [32768, 8], P(('tok', 'tp')), may hold values from 0.1 to 1
- w_gate_up: bfloat16 [32, 1024, 1024], P('tp', 'tok'), may hold values from -0.1875 to 0.1875
- w_down: bfloat16 [32, 512, 1024], P('tp', 'tok'), may hold values from -1 to 1
Outputs:
- layer_out: bfloat16 [32768, 1024], P(('tok', 'tp'))
Inputs may be any that keep to these rules, and one draw needn't show every extreme that they name: `page_table`: request r's entries are pages of its own tok index, rows 24 * (r // 2) to 24 * (r // 2 + 1) - 1; its first 8 entries are the same for all requests of that tok index, and all other entries name pages that no other entry names. `cached_len`: some request has exactly 2048 cached tokens. `expert_ids`: in the rows of one device (aligned blocks of 128 rows) no expert is named by more than 64 rows, and a row names 8 different experts.
All inputs are finite; a program needn't handle non-finite values.
Results may differ from a plain program's by a relative error of at most 0.017.
The roundings to bfloat16 on the way count: a program that leaves them out, or rounds other values in their place, can miss the bound.
Values may be sent and summed in bfloat16 or wider, within the bound.
No kernel may reach another device: no remote copies, remote signals or barrier semaphores. Data moves between devices by JAX's collectives and lax.ppermute only.
A program may use at most 128 MiB of HBM per device.

v0:
```python
import jax
import jax.numpy as jnp
from jax import lax
from jax.sharding import PartitionSpec as P

D = 1024
HEADS = 16
KV_HEADS = 8
HEAD_DIM = 64
EXPERTS = 32
FF_EXPERT = 512
TOP = 8
NEW = 1024
MAX_CACHED = 2048
REQ_DEV = 2
ATTN_SCALE = 0.015625
EPSILON = 1e-06
THETA = 10000.0


def rms_norm(values, gain):
    wide = values.astype(jnp.float32)
    factor = lax.rsqrt(jnp.mean(wide * wide, axis=-1, keepdims=True) + EPSILON)
    return (wide * factor * gain).astype(jnp.bfloat16)


def rotate(values, positions):
    row_count = values.shape[0]
    shaped = values.reshape(row_count, -1, HEAD_DIM)
    half_dim = HEAD_DIM // 2
    exponent = jnp.arange(half_dim).astype(jnp.float32) * (2.0 / HEAD_DIM)
    frequency = jnp.power(THETA, -exponent)
    angles = positions.astype(jnp.float32)[:, None] * frequency[None, :]
    cosine = jnp.cos(angles)[:, None, :]
    sine_part = jnp.sin(angles)[:, None, :]
    leading = shaped[..., :half_dim]
    trailing = shaped[..., half_dim:]
    turned = jnp.concatenate(
        [leading * cosine - trailing * sine_part, trailing * cosine + leading * sine_part], axis=-1
    )
    return turned.reshape(row_count, -1)


def attend_request(queries, keys_total, values_total, length):
    block_rows = min(NEW, 512)
    key_index = jnp.arange(MAX_CACHED + NEW, dtype=jnp.int32)

    def one_block(block_start):
        block_query = lax.dynamic_slice_in_dim(queries, block_start, block_rows, 0)
        scores = (
            jnp.einsum(
                "qgpd,kgd->gpqk", block_query, keys_total, preferred_element_type=jnp.float32
            )
            * ATTN_SCALE
        )
        query_pos = block_start + jnp.arange(block_rows, dtype=jnp.int32)
        allowed = jnp.where(
            key_index[None, :] < MAX_CACHED,
            key_index[None, :] < length,
            key_index[None, :] - MAX_CACHED <= query_pos[:, None],
        )
        scores = jnp.where(allowed, scores, -1e30)
        top_score = jnp.max(scores, axis=-1, keepdims=True)
        weights = jnp.exp(scores - top_score)
        probs = (weights / jnp.sum(weights, axis=-1, keepdims=True)).astype(jnp.bfloat16)
        mixed = jnp.einsum(
            "gpqk,kgd->qgpd", probs, values_total, preferred_element_type=jnp.float32
        )
        return mixed.astype(jnp.bfloat16).reshape(block_rows, -1)

    starts = jnp.arange(NEW // block_rows, dtype=jnp.int32) * block_rows
    return lax.map(one_block, starts).reshape(NEW, -1)


def shards(
    hidden_states,
    first_gain,
    second_gain,
    w_query,
    w_keyval,
    w_out,
    kv_cache,
    page_table,
    cached_len,
    expert_ids,
    gate_weights,
    w_gate_up,
    w_down,
):
    gate_up_full, down_full = (
        lax.all_gather(w_gate_up, "tok", axis=1, tiled=True),
        lax.all_gather(w_down, "tok", axis=1, tiled=True),
    )
    tok_rows = hidden_states.shape[0]
    tp_size = lax.axis_size("tp")
    tp_rank = lax.axis_index("tp")
    local_heads = HEADS // tp_size
    group_size = HEADS // KV_HEADS
    local_kv = max(local_heads // group_size, 1)
    per_group = local_heads // local_kv
    head_width = local_heads * HEAD_DIM
    kv_width = local_kv * HEAD_DIM
    kv_cols = KV_HEADS * HEAD_DIM
    group_tokens = REQ_DEV * NEW
    first_kv = tp_rank * local_heads // group_size
    request_range = jnp.arange(REQ_DEV, dtype=jnp.int32)
    normed = rms_norm(hidden_states, first_gain)
    key_part = lax.dynamic_slice_in_dim(w_keyval, first_kv * HEAD_DIM, kv_width, 1)
    value_part = lax.dynamic_slice_in_dim(w_keyval, kv_cols + first_kv * HEAD_DIM, kv_width, 1)
    piece = lax.all_gather(normed, "tp", axis=0, tiled=True)
    row_index = jnp.arange(piece.shape[0], dtype=jnp.int32)
    owner = row_index // NEW
    base_len = jnp.sum(
        jnp.where(owner[:, None] == request_range[None, :], cached_len[None, :], 0), axis=1
    )
    piece_pos = base_len + row_index % NEW
    query_rows = rotate(jnp.dot(piece, w_query, preferred_element_type=jnp.float32), piece_pos)
    key_rows = rotate(jnp.dot(piece, key_part, preferred_element_type=jnp.float32), piece_pos)
    value_rows = jnp.dot(piece, value_part, preferred_element_type=jnp.float32)
    projected = jnp.concatenate([query_rows, key_rows, value_rows], axis=1).astype(jnp.bfloat16)
    queries = projected[:, :head_width].reshape(REQ_DEV, NEW, local_kv, per_group, HEAD_DIM)
    new_keys = projected[:, head_width : head_width + kv_width].reshape(
        REQ_DEV, NEW, local_kv, HEAD_DIM
    )
    new_values = projected[:, head_width + kv_width :].reshape(REQ_DEV, NEW, local_kv, HEAD_DIM)
    cache_keys = lax.dynamic_slice_in_dim(kv_cache, first_kv * HEAD_DIM, kv_width, 2)
    cache_values = lax.dynamic_slice_in_dim(kv_cache, kv_cols + first_kv * HEAD_DIM, kv_width, 2)
    local_pages = page_table - lax.axis_index("tok") * kv_cache.shape[0]

    def per_request(inputs):
        page_ids, length, request_q, request_k, request_v = inputs
        keys_total = jnp.concatenate(
            [
                jnp.take(cache_keys, page_ids, axis=0).reshape(MAX_CACHED, local_kv, HEAD_DIM),
                request_k,
            ],
            axis=0,
        )
        values_total = jnp.concatenate(
            [
                jnp.take(cache_values, page_ids, axis=0).reshape(MAX_CACHED, local_kv, HEAD_DIM),
                request_v,
            ],
            axis=0,
        )
        return attend_request(request_q, keys_total, values_total, length)

    attended = lax.map(
        per_request, (local_pages, cached_len, queries, new_keys, new_values)
    ).reshape(group_tokens, head_width)
    projected_out = lax.psum_scatter(
        jnp.dot(attended, w_out, preferred_element_type=jnp.float32),
        "tp",
        scatter_dimension=0,
        tiled=True,
    )
    middle = (hidden_states.astype(jnp.float32) + projected_out).astype(jnp.bfloat16)
    normed_two = rms_norm(middle, second_gain)
    experts_local = EXPERTS // tp_size
    capacity = 2 * tok_rows * TOP // EXPERTS
    expert_range = jnp.arange(EXPERTS, dtype=jnp.int32)
    onehot = (expert_ids[:, :, None] == expert_range[None, None, :]).astype(jnp.int32)
    per_token = jnp.sum(onehot, axis=1)
    earlier = jnp.cumsum(per_token, axis=0) - per_token
    slot_ids = jnp.sum(onehot * earlier[:, None, :], axis=2)
    target = expert_ids * capacity + slot_ids
    outgoing_rows = jnp.broadcast_to(normed_two[:, None, :], (tok_rows, TOP, D))
    send_buffer = jnp.zeros((EXPERTS * capacity, D), jnp.bfloat16).at[target].set(outgoing_rows)
    received = lax.all_to_all(
        send_buffer.reshape(tp_size, experts_local, capacity, D),
        "tp",
        split_axis=0,
        concat_axis=2,
        tiled=True,
    )
    received = received.reshape(experts_local, tp_size * capacity, D)
    both = jnp.einsum("esd,edf->esf", received, gate_up_full, preferred_element_type=jnp.float32)
    activated = (jax.nn.silu(both[..., :FF_EXPERT]) * both[..., FF_EXPERT:]).astype(jnp.bfloat16)
    produced = jnp.einsum(
        "esf,efd->esd", activated, down_full, preferred_element_type=jnp.float32
    ).astype(jnp.bfloat16)
    returned = lax.all_to_all(
        produced.reshape(experts_local, tp_size, capacity, D),
        "tp",
        split_axis=1,
        concat_axis=0,
        tiled=True,
    )
    returned = returned.reshape(EXPERTS * capacity, D)
    picked = returned[target]
    mixture = jnp.einsum("tk,tkd->td", gate_weights, picked.astype(jnp.float32))
    return (middle.astype(jnp.float32) + mixture).astype(jnp.bfloat16)


def solution(mesh):
    in_specs = (
        P(("tok", "tp"), None),
        P(),
        P(),
        P(None, "tp"),
        P(),
        P("tp", None),
        P("tok", None, None),
        P("tok", None),
        P("tok"),
        P(("tok", "tp"), None),
        P(("tok", "tp"), None),
        P("tp", "tok", None),
        P("tp", "tok", None),
    )
    out_specs = P(("tok", "tp"), None)
    return jax.shard_map(shards, mesh=mesh, in_specs=in_specs, out_specs=out_specs, check_vma=False)
```

profile of v0, /device:TPU:24, one launch (start us, length us, event | category | flops | bytes accessed | tf_op | source)
XLA Modules:
  0.0 391.7 jit_solution(955928082948849221)
XLA Ops:
  7.4 1.2 fusion.29
  8.6 1.8 fusion.31
  10.6 0.7 fusion.55
  11.3 2.8 constant_dynamic-slice_fusion.1
  14.1 55.6 %all-gather.4.cloned.1.call-done = bf16[2048,1024]{1,0:T(8,128)(2,1)} async-done(((bf16[128,1024]{1,0:T(8,128)(2,1)}), bf16[2048,1024]{1,0:T(8,128)(2,1)}) %all-gather.4.cloned.1.call-update) | async-done | bytes 4194320 | tf_op jit(solution)/shard_map/all_gather | solution.py:110
  69.7 3.8 convolution_bitcast_fusion
  73.5 1.4 convolution_bitcast_fusion.1
  74.9 1.2 fusion.50
  76.1 0.8 pad_maximum_fusion.2
  76.9 1.1 reshape.360
  78.0 0.8 copy.43
  78.8 3.7 convolution_convert_fusion.1
  82.8 44.6 %while.34 = (s32[]{:T(128)}, bf16[2,1024,64]{2,1,0:T(8,128)(2,1)}, bf16[2,1024,1,1,64]{1,4,3,2,0:T(8,128)(2,1)}, s32[2,16]{1,0:T(2,128)S(1)}, bf16[24,128,64]{2,...) while((s32[]{:T(128)}, bf16[2,1024,64]{2,1,0:T(8,128)(2,1)}, ...), condition=%wide.region_7.9_spmd, body=%wide.region_2.8_spmd.sunk | while | flops 420259424 | bytes 28236604 | solution.py:148
  83.5 1.8 gather_fusion.1
  85.9 0.9 dynamic-slice_bitcast_fusion.5
  87.5 16.5 %while.35 = (s32[]{:T(128)}, bf16[2,512,64]{1,2,0:T(8,128)(2,1)S(1)}, s32[]{:T(128)}, s32[2]{0:T(128)S(1)}, bf16[1024,1,1,64]{0,3,2,1:T(8,128)(2,1)S(1)}, /*inde...) while((s32[]{:T(128)}, ...), condition=%wide.region_6.7_spmd.clone.clone, body=%wide.region_3.6_spmd.clone.clone.sunk | while | flops 418423296 | bytes 19843236 | solution.py:72
  91.3 2.0 fusion.89
  93.3 1.0 fusion.90
  94.3 1.4 fusion.91
  99.6 2.0 fusion.89
  101.5 1.0 fusion.90
  102.5 1.4 fusion.91
  104.2 0.8 copy-done.5
  105.7 1.8 gather_fusion.1
  108.2 0.9 dynamic-slice_bitcast_fusion.5
  109.7 16.5 %while.35 = (s32[]{:T(128)}, bf16[2,512,64]{1,2,0:T(8,128)(2,1)S(1)}, s32[]{:T(128)}, s32[2]{0:T(128)S(1)}, bf16[1024,1,1,64]{0,3,2,1:T(8,128)(2,1)S(1)}, /*inde...) while((s32[]{:T(128)}, ...), condition=%wide.region_6.7_spmd.clone.clone, body=%wide.region_3.6_spmd.clone.clone.sunk | while | flops 418423296 | bytes 19843236 | solution.py:72
  113.6 2.0 fusion.89
  115.5 1.0 fusion.90
  116.5 1.4 fusion.91
  121.8 2.0 fusion.89
  123.8 1.0 fusion.90
  124.8 1.4 fusion.91
  126.5 0.8 copy-done.5
  127.3 5.5 %fusion.70 = f32[2048,1024]{1,0:T(8,128)} fusion(bf16[2048,64]{1,0:T(8,128)(2,1)} %bitcast.130, bf16[64,1024]{1,0:T(8,128)(2,1)S(1)} %copy-done.6), kind=kOutput, calls=%fused_computation.117 | convolution fusion | flops 268435456 | bytes 8781824 | tf_op jit(solution)/shard_map/dot_general | solution.py:152
  134.1 89.1 %reduce-scatter.2.cloned.1.call-done = f32[128,1024]{1,0:T(8,128)} async-done(((f32[2048,1024]{1,0:T(8,128)}), f32[128,1024]{1,0:T(8,128)}) %reduce-scatter.2.cloned.1.call-update) | async-done | bytes 524304 | tf_op jit(solution)/shard_map/reduce_scatter | solution.py:151
  223.2 1.2 fusion.33
  224.5 7.9 %scatter_custom_fusion = bf16[2048,1024]{1,0:T(8,128)(2,1)} fusion(s32[1024]{0:T(1024)S(1)} %reshape.399, bf16[]{:T(256)} %constant.161.clone.1, bf16[128,1024]{1,0:T(8,128)(2,1)S(1)} %fusion.35), kind=kCustom, calls=%fused_computation.45 | custom fusion | bytes 4456450 | tf_op jit(solution)/shard_map/scatter | solution.py:168
  232.5 5.6 %all-to-all-start = ((bf16[16,2,64,1024]{3,2,1,0:T(8,128)(2,1)}), bf16[16,2,64,1024]{3,2,1,0:T(8,128)(2,1)}, u32[]{:S(2)}, u32[]{:S(2)}) async-start(bf16[16,2,64,1024]{3,2,1,0:T(8,128)(2,1)} %bitcast.126), calls=%async_computation.1 | async-start | bytes 8388608 | tf_op jit(solution)/shard_map/all_to_all | solution.py:169
  238.7 51.2 %all-to-all-done = bf16[16,2,64,1024]{3,2,1,0:T(8,128)(2,1)} async-done(((bf16[16,2,64,1024]{3,2,1,0:T(8,128)(2,1)}), bf16[16,2,64,1024]{3,2,1,0:T(8,128)(2,1)}, u32[]{:S(2)}, u32[]{:S(2)}) %all-to-all-start) | async-done | bytes 4194336 | tf_op jit(solution)/shard_map/all_to_all | solution.py:169
  289.8 4.8 %copy.50 = bf16[1,2,16,64,1024]{4,3,2,1,0:T(8,128)(2,1)} copy(bf16[1,2,16,64,1024]{4,3,1,2,0:T(8,128)(2,1)} %bitcast.14) | data formatting | bytes 8388608 | tf_op jit(solution)/shard_map/all_to_all | solution.py:169
  294.7 11.2 %fusion.71 = f32[2,1024,1024]{2,1,0:T(8,128)} fusion(bf16[2,1024,1024]{2,1,0:T(8,128)(2,1)} %bitcast.127, bf16[2,1024,1024]{2,1,0:T(8,128)(2,1)} %all-gather.6.cloned.1.call-done), kind=kOutput, calls=%fused_computation.118 | convolution fusion | flops 4294967296 | bytes 16777216 | tf_op jit(solution)/shard_map/esd,edf->esf/dot_general | solution.py:177
  305.9 6.4 %convolution_convert_fusion = bf16[2,1024,1024]{2,1,0:T(8,128)(2,1)S(1)} fusion(bf16[2,512,1024]{2,1,0:T(8,128)(2,1)} %all-gather.8.cloned.1.call-done, f32[2,1024,1024]{2,1,0:T(8,128)} %fusion.71), kind=kOutput, calls=%fused_computation.39 | convolution fusion | flops 2155872256 | bytes 14680064 | tf_op jit(solution)/shard_map/esf,efd->esd/dot_general | solution.py:179
  312.3 2.4 copy.51
  314.7 7.2 %all-to-all-start.1 = ((bf16[2,16,64,1024]{3,2,0,1:T(8,128)(2,1)}), bf16[2,16,64,1024]{3,2,0,1:T(8,128)(2,1)}, u32[]{:S(2)}, u32[]{:S(2)}) async-start(bf16[2,16,64,1024]{3,2,0,1:T(8,128)(2,1)} %copy.51), calls=%async_computation.2 | async-start | bytes 8388608 | tf_op jit(solution)/shard_map/all_to_all | solution.py:182
  322.1 50.2 %all-to-all-done.1 = bf16[2,16,64,1024]{3,2,0,1:T(8,128)(2,1)} async-done(((bf16[2,16,64,1024]{3,2,0,1:T(8,128)(2,1)}), bf16[2,16,64,1024]{3,2,0,1:T(8,128)(2,1)}, u32[]{:S(2)}, u32[]{:S(2)}) %all-to-all-start.1) | async-done | bytes 4194336 | tf_op jit(solution)/shard_map/all_to_all | solution.py:182
  372.3 8.9 %gather_fusion.2 = bf16[1024,1024]{1,0:T(8,128)(2,1)} fusion(bf16[2048,1024]{1,0:T(8,128)(2,1)} %bitcast.19, s32[1024]{0:T(1024)S(1)} %broadcast_clamp_fusion), kind=kCustom, calls=%fused_computation.2 | custom fusion | bytes 4198400 | tf_op jit(solution)/shard_map/gather | solution.py:190
  381.2 2.3 fusion.22
  383.5 0.8 fusion.36
  (104 shorter events, 14.4 us)
Async XLA Ops:
  7.4 62.3 %copy-start = (bf16[1024,1024]{1,0:T(8,128)(2,1)S(1)}, bf16[1024,1024]{1,0:T(8,128)(2,1)}, u32[]{:S(2)}) copy-start(bf16[1024,1024]{1,0:T(8,128)(2,1)} %param.23) | copy-start | bytes 6291460
  7.4 6.7 %copy-start.11 = (s32[2,16]{1,0:T(2,128)S(1)}, s32[2,16]{1,0:T(2,128)}, u32[]{:S(2)}) copy-start(s32[2,16]{1,0:T(2,128)} %param.26) | copy-start | bytes 388
  7.4 62.3 %all-gather.4.cloned.1.call-start = ((), (), s32[]{:S(2)}) async-start(), calls=%async_computation.3 | async-start | bytes 4456448 | tf_op jit(solution)/shard_map/all_gather | solution.py:110
  10.4 212.7 %reduce-scatter.2.cloned.1.call-start = ((), (), s32[]{:S(2)}) async-start(), calls=%async_computation.4 | async-start | bytes 8912896 | tf_op jit(solution)/shard_map/reduce_scatter | solution.py:151
  14.1 59.4 %copy-start.7 = (bf16[1024,64]{0,1:T(8,128)(2,1)S(1)}, bf16[1024,64]{0,1:T(8,128)(2,1)}, u32[]{:S(2)}) copy-start(bf16[1024,64]{0,1:T(8,128)(2,1)} %param.22) | copy-start | bytes 393220
  69.7 3.8 copy-start.2
  78.8 3.9 %copy-start.12 = (s32[2]{0:T(128)S(1)}, s32[2]{0:T(128)}, u32[]{:S(2)}) copy-start(s32[2]{0:T(128)} %param.27) | copy-start | bytes 28
  82.7 44.6 %copy-start.6 = (bf16[64,1024]{1,0:T(8,128)(2,1)S(1)}, bf16[64,1024]{1,0:T(8,128)(2,1)}, u32[]{:S(2)}) copy-start(bf16[64,1024]{1,0:T(8,128)(2,1)} %param.24) | copy-start | bytes 393220
  87.5 16.7 %copy-start.4 = (bf16[2,1024,64]{2,1,0:T(8,128)(2,1)S(1)}, bf16[2,1024,64]{2,1,0:T(8,128)(2,1)}, u32[]{:S(2)}) copy-start(bf16[2,1024,64]{2,1,0:T(8,128)(2,1)} %get-tuple-element.550) | copy-start | bytes 786436 | tf_op jit(solution)/shard_map/while
  104.2 0.8 copy-start.5
  109.7 16.7 %copy-start.4 = (bf16[2,1024,64]{2,1,0:T(8,128)(2,1)S(1)}, bf16[2,1024,64]{2,1,0:T(8,128)(2,1)}, u32[]{:S(2)}) copy-start(bf16[2,1024,64]{2,1,0:T(8,128)(2,1)} %get-tuple-element.550) | copy-start | bytes 786436 | tf_op jit(solution)/shard_map/while
  126.5 0.8 copy-start.5
  132.8 0.7 copy-start.8
  132.8 90.4 %copy-start.3 = (bf16[128,1024]{1,0:T(8,128)(2,1)S(1)}, bf16[128,1024]{1,0:T(8,128)(2,1)}, u32[]{:S(2)}) copy-start(bf16[128,1024]{1,0:T(8,128)(2,1)} %param.19) | copy-start | bytes 786436
  132.8 91.6 %copy-start.9 = (f32[1024]{0:T(1024)S(1)}, f32[1024]{0:T(1024)}, u32[]{:S(2)}) copy-start(f32[1024]{0:T(1024)} %param.21) | copy-start | bytes 12292
  132.8 161.8 %all-gather.6.cloned.1.call-start = ((), (), s32[]{:S(2)}) async-start(), calls=%async_computation.5 | async-start | bytes 4456448 | tf_op jit(solution)/shard_map/all_gather | solution.py:91
  232.5 57.4 %all-to-all-start = ((bf16[16,2,64,1024]{3,2,1,0:T(8,128)(2,1)}), bf16[16,2,64,1024]{3,2,1,0:T(8,128)(2,1)}, u32[]{:S(2)}, u32[]{:S(2)}) async-start(bf16[16,2,64,1024]{3,2,1,0:T(8,128)(2,1)} %bitcast.126), calls=%async_computation.1 | async-start | bytes 8388608 | tf_op jit(solution)/shard_map/all_to_all | solution.py:169
  238.1 67.8 %all-gather.8.cloned.1.call-start = ((), (), s32[]{:S(2)}) async-start(), calls=%async_computation.6 | async-start | bytes 2228224 | tf_op jit(solution)/shard_map/all_gather | solution.py:92
  314.7 7.2 %copy-start.10 = (f32[128,8]{0,1:T(8,128)S(1)}, f32[128,8]{0,1:T(8,128)}, u32[]{:S(2)}) copy-start(f32[128,8]{0,1:T(8,128)} %param.29) | copy-start | bytes 12292
  314.7 57.5 %all-to-all-start.1 = ((bf16[2,16,64,1024]{3,2,0,1:T(8,128)(2,1)}), bf16[2,16,64,1024]{3,2,0,1:T(8,128)(2,1)}, u32[]{:S(2)}, u32[]{:S(2)}) async-start(bf16[2,16,64,1024]{3,2,0,1:T(8,128)(2,1)} %copy.51), calls=%async_computation.2 | async-start | bytes 8388608 | tf_op jit(solution)/shard_map/all_to_all | solution.py:182
  372.3 12.0 %copy-start.1 = (bf16[1024,1024]{1,0:T(8,128)(2,1)S(1)}, bf16[1024,1024]{1,0:T(8,128)(2,1)}, u32[]{:S(2)}) copy-start(bf16[1024,1024]{1,0:T(8,128)(2,1)} %param.23) | copy-start | bytes 6291460
Sparse Core Ops, SparseCore 0:
  10.6 59.0 all-gather.3
  133.0 90.1 reduce-scatter.1
Sparse Core Ops, SparseCore 1:
  135.2 41.6 all-gather.5
  240.4 40.7 all-gather.7
where the time goes:
time: 393 us; the launch traced here: 392 us
  waiting for transfers between devices  247 us (63%)
  matrix products  47.9 us (12%)
  local copies, waits for them, and re-layouts  43 us (11%)
  other arithmetic  17.8 us (5%)
  between operations  15.1 us (4%)
  starting transfers between devices  13.1 us (3%)
  loops' own time  7.97 us (2%)
    reduce_scatter x1, waiting for transfers between devices, shards(): lax.psum_scatter(jnp.dot(attended, w_out, preferred_element_type=jnp.floa...  89.1 us
    all_gather x1, waiting for transfers between devices, shards(): piece = lax.all_gather(normed, 'tp', axis=0, tiled=True)  55.6 us
    all_to_all x1, waiting for transfers between devices, shards(): lax.all_to_all(send_buffer.reshape(tp_size, experts_local, capacity, D),...  51.2 us
    all_to_all x1, waiting for transfers between devices, shards(): lax.all_to_all(produced.reshape(experts_local, tp_size, capacity, D), 'tp...  50.2 us
    dot_general x1, matrix products, shards(): jnp.einsum('esd,edf->esf', received, gate_up_full, preferred_element_type...  11.2 us
    gather x1, local copies, waits for them, and re-layouts, shards(): picked = returned[target]  8.89 us
    scatter x1, local copies, waits for them, and re-layouts, shards(): jnp.zeros((EXPERTS * capacity, D), jnp.bfloat16).at[target]  7.92 us
    dot_general x4, matrix products, one_block(): jnp.einsum('qgpd,kgd->gpqk', block_query, keys_total, preferred_element_t...  7.91 us
  transfers between devices with their start and end apart: 6, of which 4 were waited for; matrix products, arithmetic and copies ran while one was open for 8% of the time, Pallas kernels for 0%

commit v1 on v0

--- a/solution.py
+++ b/solution.py
@@ -107,7 +107,9 @@
     normed = rms_norm(hidden_states, first_gain)
     key_part = lax.dynamic_slice_in_dim(w_keyval, first_kv * HEAD_DIM, kv_width, 1)
     value_part = lax.dynamic_slice_in_dim(w_keyval, kv_cols + first_kv * HEAD_DIM, kv_width, 1)
-    piece = lax.all_gather(normed, "tp", axis=0, tiled=True)
+    piece = jnp.concatenate(
+        lax.all_to_all(jnp.stack([normed] * lax.axis_size("tp")), "tp", 0, 0), axis=0
+    )
     row_index = jnp.arange(piece.shape[0], dtype=jnp.int32)
     owner = row_index // NEW
     base_len = jnp.sum(

time: 393 us -> 411 us (1.046)
  waiting for transfers between devices: 247 us -> 257 us
  starting transfers between devices: 13.1 us -> 20.5 us
    all_gather x1 -> x0, waiting for transfers between devices: 55.6 us -> none  [shards(): piece = lax.all_gather(normed, 'tp', axis=0, tiled=True)]
    all_to_all x0 -> x1, waiting for transfers between devices: none -> 52.6 us  [shards(): lax.all_to_all(jnp.stack([normed] * lax.axis_size('tp')), 'tp', 0, 0)]
    reduce_scatter x1, waiting for transfers between devices: 89.1 us -> 102 us  [shards(): lax.psum_scatter(jnp.dot(attended, w_out, preferred_element_type=jnp.floa...]
    all_to_all x0 -> x1, starting transfers between devices: none -> 7.3 us  [shards(): lax.all_to_all(jnp.stack([normed] * lax.axis_size('tp')), 'tp', 0, 0)]
  transfers between devices with their start and end apart: 6 -> 6, of which waited for: 4 -> 4; matrix products, arithmetic and copies ran while one was open for 8% -> 7% of each run, Pallas kernels for 0% -> 0%
where the time goes in v1:
time: 411 us; the launch traced here: 410 us
  waiting for transfers between devices  257 us (63%)
  matrix products  50 us (12%)
  local copies, waits for them, and re-layouts  44.5 us (11%)
  starting transfers between devices  20.5 us (5%)
  other arithmetic  15.7 us (4%)
  between operations  15.1 us (4%)
  loops' own time  8.03 us (2%)
    reduce_scatter x1, waiting for transfers between devices, shards(): lax.psum_scatter(jnp.dot(attended, w_out, preferred_element_type=jnp.floa...  102 us
    all_to_all x1, waiting for transfers between devices, shards(): lax.all_to_all(jnp.stack([normed] * lax.axis_size('tp')), 'tp', 0, 0)  52.6 us
    all_to_all x1, waiting for transfers between devices, shards(): lax.all_to_all(send_buffer.reshape(tp_size, experts_local, capacity, D),...  51 us
    all_to_all x1, waiting for transfers between devices, shards(): lax.all_to_all(produced.reshape(experts_local, tp_size, capacity, D), 'tp...  50.1 us
    dot_general x1, matrix products, shards(): jnp.einsum('esd,edf->esf', received, gate_up_full, preferred_element_type...  11.2 us
    gather x1, local copies, waits for them, and re-layouts, shards(): picked = returned[target]  8.9 us
  transfers between devices with their start and end apart: 6, of which 4 were waited for; matrix products, arithmetic and copies ran while one was open for 7% of the time, Pallas kernels for 0%

profile of v1, /device:TPU:24, one launch (start us, length us, event | category | flops | bytes accessed | tf_op | source)
XLA Modules:
  0.0 410.4 jit_solution(3162848735946489916)
XLA Ops:
  7.4 1.2 fusion.29
  8.6 1.1 fusion.31
  9.7 2.5 stack.2
  12.2 7.3 %all-to-all-start = ((bf16[16,128,1024]{2,1,0:T(8,128)(2,1)}), bf16[16,128,1024]{2,1,0:T(8,128)(2,1)}, u32[]{:S(2)}, u32[]{:S(2)}) async-start(bf16[16,128,1024]{2,1,0:T(8,128)(2,1)} %stack.2), calls=%async_computation | async-start | bytes 8388608 | tf_op jit(solution)/shard_map/all_to_all | solution.py:111
  19.7 2.8 constant_dynamic-slice_fusion.1
  22.6 52.6 %all-to-all-done = bf16[16,128,1024]{2,1,0:T(8,128)(2,1)} async-done(((bf16[16,128,1024]{2,1,0:T(8,128)(2,1)}), bf16[16,128,1024]{2,1,0:T(8,128)(2,1)}, u32[]{:S(2)}, u32[]{:S(2)}) %all-to-all-start) | async-done | bytes 4194336 | tf_op jit(solution)/shard_map/all_to_all | solution.py:111
  75.2 3.6 convolution_bitcast_fusion
  78.9 3.7 convolution_convert_fusion.1
  82.6 3.6 convolution_bitcast_fusion.1
  86.2 1.2 fusion.50
  87.6 0.8 copy.43
  88.7 44.5 %while.34 = (s32[]{:T(128)}, bf16[2,1024,64]{2,1,0:T(8,128)(2,1)}, bf16[2,1024,1,1,64]{1,4,3,2,0:T(8,128)(2,1)}, s32[2,16]{1,0:T(2,128)S(1)}, bf16[24,128,64]{2,...) while((s32[]{:T(128)}, bf16[2,1024,64]{2,1,0:T(8,128)(2,1)}, ...), condition=%wide.region_7.9_spmd, body=%wide.region_2.8_spmd.sunk | while | flops 420259424 | bytes 28236604 | solution.py:150
  89.4 1.8 gather_fusion.1
  91.8 0.9 dynamic-slice_bitcast_fusion.5
  93.4 16.5 %while.35 = (s32[]{:T(128)}, bf16[2,512,64]{1,2,0:T(8,128)(2,1)S(1)}, s32[]{:T(128)}, s32[2]{0:T(128)S(1)}, bf16[1024,1,1,64]{0,3,2,1:T(8,128)(2,1)S(1)}, /*inde...) while((s32[]{:T(128)}, ...), condition=%wide.region_6.7_spmd.clone.clone, body=%wide.region_3.6_spmd.clone.clone.sunk | while | flops 418423296 | bytes 19843236 | solution.py:72
  97.2 2.0 fusion.89
  99.2 1.0 fusion.90
  100.2 1.4 fusion.91
  105.5 2.0 fusion.89
  107.4 1.0 fusion.90
  108.4 1.4 fusion.91
  110.1 0.8 copy-done.4
  111.0 0.6 gather_fusion
  111.6 1.8 gather_fusion.1
  114.1 0.9 dynamic-slice_bitcast_fusion.5
  115.6 16.5 %while.35 = (s32[]{:T(128)}, bf16[2,512,64]{1,2,0:T(8,128)(2,1)S(1)}, s32[]{:T(128)}, s32[2]{0:T(128)S(1)}, bf16[1024,1,1,64]{0,3,2,1:T(8,128)(2,1)S(1)}, /*inde...) while((s32[]{:T(128)}, ...), condition=%wide.region_6.7_spmd.clone.clone, body=%wide.region_3.6_spmd.clone.clone.sunk | while | flops 418423296 | bytes 19843236 | solution.py:72
  119.4 2.0 fusion.89
  121.4 1.0 fusion.90
  122.4 1.4 fusion.91
  127.7 2.0 fusion.89
  129.7 1.0 fusion.90
  130.7 1.4 fusion.91
  132.4 0.8 copy-done.4
  133.2 5.5 %fusion.70 = f32[2048,1024]{1,0:T(8,128)} fusion(bf16[2048,64]{1,0:T(8,128)(2,1)} %bitcast.131, bf16[64,1024]{1,0:T(8,128)(2,1)S(1)} %copy-done.5), kind=kOutput, calls=%fused_computation.117 | convolution fusion | flops 268435456 | bytes 8781824 | tf_op jit(solution)/shard_map/dot_general | solution.py:154
  140.0 101.9 %reduce-scatter.2.cloned.1.call-done = f32[128,1024]{1,0:T(8,128)} async-done(((f32[2048,1024]{1,0:T(8,128)}), f32[128,1024]{1,0:T(8,128)}) %reduce-scatter.2.cloned.1.call-update) | async-done | bytes 524304 | tf_op jit(solution)/shard_map/reduce_scatter | solution.py:153
  241.9 1.2 fusion.33
  243.3 7.9 %scatter_custom_fusion = bf16[2048,1024]{1,0:T(8,128)(2,1)} fusion(s32[1024]{0:T(1024)S(1)} %reshape.405, bf16[]{:T(256)} %constant.161.clone.1, bf16[128,1024]{1,0:T(8,128)(2,1)S(1)} %fusion.35), kind=kCustom, calls=%fused_computation.45 | custom fusion | bytes 4456450 | tf_op jit(solution)/shard_map/scatter | solution.py:170
  251.2 5.7 %all-to-all-start.1 = ((bf16[16,2,64,1024]{3,2,1,0:T(8,128)(2,1)}), bf16[16,2,64,1024]{3,2,1,0:T(8,128)(2,1)}, u32[]{:S(2)}, u32[]{:S(2)}) async-start(bf16[16,2,64,1024]{3,2,1,0:T(8,128)(2,1)} %bitcast.127), calls=%async_computation.2 | async-start | bytes 8388608 | tf_op jit(solution)/shard_map/all_to_all | solution.py:171
  257.5 51.0 %all-to-all-done.1 = bf16[16,2,64,1024]{3,2,1,0:T(8,128)(2,1)} async-done(((bf16[16,2,64,1024]{3,2,1,0:T(8,128)(2,1)}), bf16[16,2,64,1024]{3,2,1,0:T(8,128)(2,1)}, u32[]{:S(2)}, u32[]{:S(2)}) %all-to-all-start.1) | async-done | bytes 4194336 | tf_op jit(solution)/shard_map/all_to_all | solution.py:171
  308.5 4.8 %copy.50 = bf16[1,2,16,64,1024]{4,3,2,1,0:T(8,128)(2,1)} copy(bf16[1,2,16,64,1024]{4,3,1,2,0:T(8,128)(2,1)} %bitcast.15) | data formatting | bytes 8388608 | tf_op jit(solution)/shard_map/all_to_all | solution.py:171
  313.3 11.2 %fusion.71 = f32[2,1024,1024]{2,1,0:T(8,128)} fusion(bf16[2,1024,1024]{2,1,0:T(8,128)(2,1)} %bitcast.128, bf16[2,1024,1024]{2,1,0:T(8,128)(2,1)} %all-gather.3.cloned.1.call-done), kind=kOutput, calls=%fused_computation.118 | convolution fusion | flops 4294967296 | bytes 16777216 | tf_op jit(solution)/shard_map/esd,edf->esf/dot_general | solution.py:179
  324.5 6.4 %convolution_convert_fusion = bf16[2,1024,1024]{2,1,0:T(8,128)(2,1)S(1)} fusion(bf16[2,512,1024]{2,1,0:T(8,128)(2,1)} %all-gather.5.cloned.1.call-done, f32[2,1024,1024]{2,1,0:T(8,128)} %fusion.71), kind=kOutput, calls=%fused_computation.39 | convolution fusion | flops 2155872256 | bytes 14680064 | tf_op jit(solution)/shard_map/esf,efd->esd/dot_general | solution.py:181
  330.9 2.4 copy.51
  333.4 7.3 %all-to-all-start.2 = ((bf16[2,16,64,1024]{3,2,0,1:T(8,128)(2,1)}), bf16[2,16,64,1024]{3,2,0,1:T(8,128)(2,1)}, u32[]{:S(2)}, u32[]{:S(2)}) async-start(bf16[2,16,64,1024]{3,2,0,1:T(8,128)(2,1)} %copy.51), calls=%async_computation.3 | async-start | bytes 8388608 | tf_op jit(solution)/shard_map/all_to_all | solution.py:184
  340.8 50.1 %all-to-all-done.2 = bf16[2,16,64,1024]{3,2,0,1:T(8,128)(2,1)} async-done(((bf16[2,16,64,1024]{3,2,0,1:T(8,128)(2,1)}), bf16[2,16,64,1024]{3,2,0,1:T(8,128)(2,1)}, u32[]{:S(2)}, u32[]{:S(2)}) %all-to-all-start.2) | async-done | bytes 4194336 | tf_op jit(solution)/shard_map/all_to_all | solution.py:184
  390.9 8.9 %gather_fusion.2 = bf16[1024,1024]{1,0:T(8,128)(2,1)} fusion(bf16[2048,1024]{1,0:T(8,128)(2,1)} %bitcast.20, s32[1024]{0:T(1024)S(1)} %broadcast_clamp_fusion), kind=kCustom, calls=%fused_computation.2 | custom fusion | bytes 4198400 | tf_op jit(solution)/shard_map/gather | solution.py:192
  399.8 2.3 fusion.22
  402.1 0.8 fusion.36
  (102 shorter events, 14.0 us)
Async XLA Ops:
  7.4 67.9 %copy-start = (bf16[1024,1024]{1,0:T(8,128)(2,1)S(1)}, bf16[1024,1024]{1,0:T(8,128)(2,1)}, u32[]{:S(2)}) copy-start(bf16[1024,1024]{1,0:T(8,128)(2,1)} %param.23) | copy-start | bytes 6291460
  12.2 7.4 %copy-start.11 = (s32[2]{0:T(128)S(1)}, s32[2]{0:T(128)}, u32[]{:S(2)}) copy-start(s32[2]{0:T(128)} %param.27) | copy-start | bytes 28
  12.2 10.4 %copy-start.10 = (s32[2,16]{1,0:T(2,128)S(1)}, s32[2,16]{1,0:T(2,128)}, u32[]{:S(2)}) copy-start(s32[2,16]{1,0:T(2,128)} %param.26) | copy-start | bytes 388
  12.2 63.0 %all-to-all-start = ((bf16[16,128,1024]{2,1,0:T(8,128)(2,1)}), bf16[16,128,1024]{2,1,0:T(8,128)(2,1)}, u32[]{:S(2)}, u32[]{:S(2)}) async-start(bf16[16,128,1024]{2,1,0:T(8,128)(2,1)} %stack.2), calls=%async_computation | async-start | bytes 8388608 | tf_op jit(solution)/shard_map/all_to_all | solution.py:111
  19.5 222.4 %reduce-scatter.2.cloned.1.call-start = ((), (), s32[]{:S(2)}) async-start(), calls=%async_computation.4 | async-start | bytes 8912896 | tf_op jit(solution)/shard_map/reduce_scatter | solution.py:153
  78.9 3.7 copy-start.6
  88.6 44.5 %copy-start.5 = (bf16[64,1024]{1,0:T(8,128)(2,1)S(1)}, bf16[64,1024]{1,0:T(8,128)(2,1)}, u32[]{:S(2)}) copy-start(bf16[64,1024]{1,0:T(8,128)(2,1)} %param.24) | copy-start | bytes 393220
  93.4 16.7 %copy-start.3 = (bf16[2,1024,64]{2,1,0:T(8,128)(2,1)S(1)}, bf16[2,1024,64]{2,1,0:T(8,128)(2,1)}, u32[]{:S(2)}) copy-start(bf16[2,1024,64]{2,1,0:T(8,128)(2,1)} %get-tuple-element.550) | copy-start | bytes 786436 | tf_op jit(solution)/shard_map/while
  110.1 0.8 copy-start.4
  115.6 16.7 %copy-start.3 = (bf16[2,1024,64]{2,1,0:T(8,128)(2,1)S(1)}, bf16[2,1024,64]{2,1,0:T(8,128)(2,1)}, u32[]{:S(2)}) copy-start(bf16[2,1024,64]{2,1,0:T(8,128)(2,1)} %get-tuple-element.550) | copy-start | bytes 786436 | tf_op jit(solution)/shard_map/while
  132.4 0.8 copy-start.4
  138.7 0.7 copy-start.7
  138.7 103.2 %copy-start.2 = (bf16[128,1024]{1,0:T(8,128)(2,1)S(1)}, bf16[128,1024]{1,0:T(8,128)(2,1)}, u32[]{:S(2)}) copy-start(bf16[128,1024]{1,0:T(8,128)(2,1)} %param.19) | copy-start | bytes 786436
  138.7 104.4 %copy-start.8 = (f32[1024]{0:T(1024)S(1)}, f32[1024]{0:T(1024)}, u32[]{:S(2)}) copy-start(f32[1024]{0:T(1024)} %param.21) | copy-start | bytes 12292
  138.7 174.6 %all-gather.3.cloned.1.call-start = ((), (), s32[]{:S(2)}) async-start(), calls=%async_computation.5 | async-start | bytes 4456448 | tf_op jit(solution)/shard_map/all_gather | solution.py:91
  251.2 57.3 %all-to-all-start.1 = ((bf16[16,2,64,1024]{3,2,1,0:T(8,128)(2,1)}), bf16[16,2,64,1024]{3,2,1,0:T(8,128)(2,1)}, u32[]{:S(2)}, u32[]{:S(2)}) async-start(bf16[16,2,64,1024]{3,2,1,0:T(8,128)(2,1)} %bitcast.127), calls=%async_computation.2 | async-start | bytes 8388608 | tf_op jit(solution)/shard_map/all_to_all | solution.py:171
  256.9 67.6 %all-gather.5.cloned.1.call-start = ((), (), s32[]{:S(2)}) async-start(), calls=%async_computation.6 | async-start | bytes 2228224 | tf_op jit(solution)/shard_map/all_gather | solution.py:92
  333.4 7.3 %copy-start.9 = (f32[128,8]{0,1:T(8,128)S(1)}, f32[128,8]{0,1:T(8,128)}, u32[]{:S(2)}) copy-start(f32[128,8]{0,1:T(8,128)} %param.29) | copy-start | bytes 12292
  333.4 57.6 %all-to-all-start.2 = ((bf16[2,16,64,1024]{3,2,0,1:T(8,128)(2,1)}), bf16[2,16,64,1024]{3,2,0,1:T(8,128)(2,1)}, u32[]{:S(2)}, u32[]{:S(2)}) async-start(bf16[2,16,64,1024]{3,2,0,1:T(8,128)(2,1)} %copy.51), calls=%async_computation.3 | async-start | bytes 8388608 | tf_op jit(solution)/shard_map/all_to_all | solution.py:184
  390.9 12.0 %copy-start.1 = (bf16[1024,1024]{1,0:T(8,128)(2,1)S(1)}, bf16[1024,1024]{1,0:T(8,128)(2,1)}, u32[]{:S(2)}) copy-start(bf16[1024,1024]{1,0:T(8,128)(2,1)} %param.23) | copy-start | bytes 6291460
Sparse Core Ops, SparseCore 0:
  138.8 103.0 reduce-scatter.1
Sparse Core Ops, SparseCore 1:
  141.0 54.8 all-gather.2
  259.2 40.8 all-gather.4
